TPU v7x, 32 devices: a whole 2x2x4 slice. The times are simulated.
32 devices in a mesh: seq: 16 (over z, y, core), head: 2 (over x).
Axes of the slice: x: 2, y: 2, z: 4, core: 2. Of those that a mesh axis runs over, the one named last changes fastest.
Arguments:
- queries: bfloat16 [4096, 4096], P(('seq', 'head')), may hold values from -6 to 6
- keys: bfloat16 [4096, 4096], P(('seq', 'head')), may hold values from -6 to 6
- values: bfloat16 [4096, 4096], P(('seq', 'head')), may hold values from -75 to 75
- out_weight: bfloat16 [4096, 4096], P('seq', 'head'), may hold values from -0.09375 to 0.09375
- norm_gain: float32 [4096], P('head'), may hold values from 0.5 to 1.5
Outputs:
- projected: bfloat16 [4096, 4096], P('seq', 'head')
All inputs are finite; a program needn't handle non-finite values.
Results may differ from a plain program's by a relative error of at most 0.0058.
Values may be sent and summed in bfloat16 or wider, within the bound.
No kernel may reach another device: no remote copies, remote signals or barrier semaphores. Data moves between devices by JAX's collectives and lax.ppermute only.
A program may use at most 128 MiB of HBM per device.

v0:
```python
import jax
import jax.numpy as jnp
from jax import lax
from jax.sharding import PartitionSpec as P

HEAD_DIM = 128


def carried_in(part, axis, combine, identity):
    place = lax.axis_index(axis)
    gathered = lax.all_gather(part, axis)
    state = jnp.zeros_like(part) + jnp.asarray(identity, part.dtype)

    def one(hop, state):
        return combine(state, lax.dynamic_index_in_dim(gathered, hop, 0, False))

    return lax.fori_loop(0, place, one, state)


def add_states(earlier, later):
    return earlier + later


def local(queries, keys, values, out_weight, norm_gain):
    heads_dev = norm_gain.shape[0] // HEAD_DIM
    query_block, key_block, value_block = (
        lax.all_to_all(queries, "head", split_axis=1, concat_axis=0, tiled=True),
        lax.all_to_all(keys, "head", split_axis=1, concat_axis=0, tiled=True),
        lax.all_to_all(values, "head", split_axis=1, concat_axis=0, tiled=True),
    )
    row_count = query_block.shape[0]
    query_heads = query_block.reshape(row_count, heads_dev, HEAD_DIM)
    key_heads = key_block.reshape(row_count, heads_dev, HEAD_DIM)
    value_heads = value_block.reshape(row_count, heads_dev, HEAD_DIM)
    kv_state = jnp.einsum(
        "thd,the->hde", key_heads, value_heads, preferred_element_type=jnp.float32
    )
    prefix = carried_in(kv_state, "seq", add_states, jnp.zeros_like(kv_state))
    carried = jnp.einsum(
        "thd,hde->the", query_heads, prefix.astype(jnp.bfloat16), preferred_element_type=jnp.float32
    )
    block_rows = min(512, row_count)
    parts_list = []
    for first_row in range(0, row_count, block_rows):
        last_row = min(first_row + block_rows, row_count)
        scores = jnp.einsum(
            "thd,shd->hts",
            query_heads[first_row:last_row],
            key_heads[:last_row],
            preferred_element_type=jnp.float32,
        )
        row_index = first_row + lax.broadcasted_iota(jnp.int32, (last_row - first_row, last_row), 0)
        col_index = lax.broadcasted_iota(jnp.int32, (last_row - first_row, last_row), 1)
        scores = jnp.where((col_index <= row_index)[None], scores, jnp.zeros_like(scores)).astype(
            jnp.bfloat16
        )
        parts_list.append(
            jnp.einsum(
                "hts,she->the", scores, value_heads[:last_row], preferred_element_type=jnp.float32
            )
        )
    within_block = jnp.concatenate(parts_list, axis=0)
    attended = carried + within_block
    mean_square = jnp.mean(attended * attended, axis=2, keepdims=True)
    gain_heads = norm_gain.reshape(heads_dev, HEAD_DIM)
    normed = (attended * lax.rsqrt(mean_square + 1e-06) * gain_heads[None]).astype(jnp.bfloat16)
    normed = normed.reshape(row_count, heads_dev * HEAD_DIM)
    returned = lax.all_to_all(normed, "head", split_axis=0, concat_axis=1, tiled=True)
    gathered = lax.all_gather(returned, "head", axis=0, tiled=True)
    outcome = jnp.dot(
        gathered,
        lax.all_gather(out_weight, "seq", axis=0, tiled=True),
        preferred_element_type=jnp.float32,
    )
    return outcome.astype(jnp.bfloat16)


def solution(mesh):
    return jax.shard_map(
        local,
        mesh=mesh,
        in_specs=(
            P(("seq", "head"), None),
            P(("seq", "head"), None),
            P(("seq", "head"), None),
            P("seq", "head"),
            P("head"),
        ),
        out_specs=P("seq", "head"),
        check_vma=False,
    )
```

profile of v0, /device:TPU:0, one launch (start us, length us, event | category | flops | bytes accessed | tf_op | source)
XLA Modules:
  0.0 361.1 jit_solution(12308427636008386715)
XLA Ops:
  6.5 0.0 copy-start.1
  6.5 2.4 copy.44
  8.9 4.2 %all-to-all-start.1 = ((bf16[128,2,2048]{2,0,1:T(8,128)(2,1)}), bf16[128,2,2048]{2,0,1:T(8,128)(2,1)S(1)}, u32[]{:S(2)}, u32[]{:S(2)}) async-start(bf16[128,2,2048]{2,0,1:T(8,128)(2,1)} %bitcast.38), calls=%async_computation.1 | async-start | bytes 2097152 | tf_op jit(solution)/shard_map/all_to_all | solution.py:29
  13.1 0.0 copy-done.1
  13.1 1.3 copy.17
  14.4 13.1 %all-to-all-done.1 = bf16[128,2,2048]{2,0,1:T(8,128)(2,1)S(1)} async-done(((bf16[128,2,2048]{2,0,1:T(8,128)(2,1)}), bf16[128,2,2048]{2,0,1:T(8,128)(2,1)S(1)}, u32[]{:S(2)}, u32[]{:S(2)}) %all-to-all-start.1) | async-done | bytes 1048608 | tf_op jit(solution)/shard_map/all_to_all | solution.py:29
  27.6 3.6 all-to-all-start
  31.2 0.0 all-gather.9.cloned.1.call-start
  31.2 0.2 copy.32
  31.4 0.8 copy.26
  32.2 12.2 %all-to-all-done = bf16[128,2,2048]{0,2,1:T(8,128)(2,1)S(1)} async-done(((bf16[128,2,2048]{0,2,1:T(8,128)(2,1)}), bf16[128,2,2048]{0,2,1:T(8,128)(2,1)S(1)}, u32[]{:S(2)}, u32[]{:S(2)}) %all-to-all-start) | async-done | bytes 1048608 | tf_op jit(solution)/shard_map/all_to_all | solution.py:28
  44.5 8.6 %copy.18 = bf16[2,128,2048]{1,0,2:T(2,128)(2,1)S(1)} copy(bf16[2,128,2048]{1,2,0:T(8,128)(2,1)S(1)} %bitcast.44) | data formatting | bytes 2097152 | tf_op jit(solution)/shard_map/all_to_all | solution.py:28
  53.1 0.7 reshape.42
  53.8 0.0 copy-start.2
  53.8 1.4 fusion.6
  55.3 0.0 all-gather.9.cloned.1.call-update
  55.3 0.0 all-gather.7.cloned.1.call-start
  55.3 0.7 all-gather.7.cloned.1.call-update
  56.0 0.0 copy-done.2
  56.1 1.0 copy.43
  57.1 3.6 all-to-all-start.2
  60.7 0.0 all-gather.5.cloned.1.call-start
  60.8 12.3 %all-to-all-done.2 = bf16[128,2,2048]{2,0,1:T(8,128)(2,1)S(1)} async-done(((bf16[128,2,2048]{2,0,1:T(8,128)(2,1)}), bf16[128,2,2048]{2,0,1:T(8,128)(2,1)S(1)}, u32[]{:S(2)}, u32[]{:S(2)}) %all-to-all-start.2) | async-done | bytes 1048608 | tf_op jit(solution)/shard_map/all_to_all | solution.py:27
  73.1 1.2 copy.33
  74.3 3.8 %fusion = f32[16,256,128]{1,2,0:T(8,128)} fusion(bf16[256,16,128]{0,2,1:T(8,128)(2,1)S(1)} %copy.26, bf16[256,16,128]{0,2,1:T(8,128)(2,1)S(1)} %reshape.42, pred[256,256]{1,0:T(8,128)(4,1)S(1)} %iota_compare_fusion, bf16[256,16,128]{2,1,0:T(8,128)(2,1)} %bitcast.47), kind=kOutput, calls=%fused_computation.6 | convolution fusion | flops 538968064 | bytes 5308416 | tf_op jit(solution)/shard_map/hts,she->the/dot_general | solution.py:58
  78.1 104.5 %all-gather.9.cloned.1.call-done = f32[256,128,128]{2,1,0:T(8,128)} async-done(((f32[16,128,128]{2,1,0:T(8,128)}), f32[256,128,128]{2,1,0:T(8,128)}) %all-gather.9.cloned.1.call-update) | async-done | bytes 16777232 | tf_op jit(solution)/shard_map/all_gather | solution.py:11
  182.6 0.1 broadcast_in_dim.16
  182.7 0.0 copy-start
  182.7 1.2 copy-done
  183.9 0.0 copy-start.3
  183.9 2.2 multiply_reduce_fusion
  186.1 0.0 copy-done.3
  186.2 0.3 multiply_convert_fusion
  186.5 0.3 all_to_all.59
  186.8 0.1 copy.27
  186.9 17.9 %all_to_all.67 = bf16[2,128,2048]{1,2,0:T(8,128)(2,1)} all-to-all(bf16[2,128,2048]{1,2,0:T(8,128)(2,1)S(1)} %copy.27), channel_id=1, replica_groups=mesh['seq'=16,'head'=2] {'head'}, dimensions={0} | all-to-all | bytes 2097152 | tf_op jit(solution)/shard_map/all_to_all | solution.py:68
  204.9 0.0 all-gather.5.cloned.1.call-update
  204.9 104.9 %all-gather.7.cloned.1.call-done = bf16[4096,2048]{1,0:T(8,128)(2,1)} async-done(((bf16[256,2048]{1,0:T(8,128)(2,1)}), bf16[4096,2048]{1,0:T(8,128)(2,1)}) %all-gather.7.cloned.1.call-update) | async-done | bytes 16777232 | tf_op jit(solution)/shard_map/all_gather | solution.py:72
  309.9 32.8 %all-gather.5.cloned.1.call-done = bf16[256,4096]{0,1:T(8,128)(2,1)} async-done(((bf16[128,4096]{0,1:T(8,128)(2,1)}), bf16[256,4096]{0,1:T(8,128)(2,1)}) %all-gather.5.cloned.1.call-update) | async-done | bytes 2097168 | tf_op jit(solution)/shard_map/all_gather | solution.py:69
  342.7 11.9 %convolution_convert_fusion = bf16[256,2048]{1,0:T(8,128)(2,1)} fusion(bf16[256,4096]{0,1:T(8,128)(2,1)} %all-gather.5.cloned.1.call-done, bf16[4096,2048]{1,0:T(8,128)(2,1)} %all-gather.7.cloned.1.call-done), kind=kOutput, calls=%fused_computation.2 | convolution fusion | flops 4295491584 | bytes 19922944 | tf_op jit(solution)/shard_map/dot_general | solution.py:70
  (3 shorter events, 0.0 us)
Async XLA Ops:
  6.5 6.6 %copy-start.1 = (bf16[128,4096]{1,0:T(8,128)(2,1)S(1)}, bf16[128,4096]{1,0:T(8,128)(2,1)}, u32[]{:S(2)}) copy-start(bf16[128,4096]{1,0:T(8,128)(2,1)} %param.8) | copy-start | bytes 3145732
  8.9 18.6 %all-to-all-start.1 = ((bf16[128,2,2048]{2,0,1:T(8,128)(2,1)}), bf16[128,2,2048]{2,0,1:T(8,128)(2,1)S(1)}, u32[]{:S(2)}, u32[]{:S(2)}) async-start(bf16[128,2,2048]{2,0,1:T(8,128)(2,1)} %bitcast.38), calls=%async_computation.1 | async-start | bytes 2097152 | tf_op jit(solution)/shard_map/all_to_all | solution.py:29
  27.6 16.9 %all-to-all-start = ((bf16[128,2,2048]{0,2,1:T(8,128)(2,1)}), bf16[128,2,2048]{0,2,1:T(8,128)(2,1)S(1)}, u32[]{:S(2)}, u32[]{:S(2)}) async-start(bf16[128,2,2048]{0,2,1:T(8,128)(2,1)} %bitcast.1), calls=%async_computation | async-start | bytes 2097152 | tf_op jit(solution)/shard_map/all_to_all | solution.py:28
  31.2 151.4 %all-gather.9.cloned.1.call-start = ((), (), s32[]{:S(2)}) async-start(), calls=%async_computation.6 | async-start | bytes 17825792 | tf_op jit(solution)/shard_map/all_gather | solution.py:11
  53.8 2.2 copy-start.2
  55.3 254.6 %all-gather.7.cloned.1.call-start = ((), (), s32[]{:S(2)}) async-start(), calls=%async_computation.5 | async-start | bytes 17825792 | tf_op jit(solution)/shard_map/all_gather | solution.py:72
  57.1 16.0 %all-to-all-start.2 = ((bf16[128,2,2048]{2,0,1:T(8,128)(2,1)}), bf16[128,2,2048]{2,0,1:T(8,128)(2,1)S(1)}, u32[]{:S(2)}, u32[]{:S(2)}) async-start(bf16[128,2,2048]{2,0,1:T(8,128)(2,1)} %bitcast.43), calls=%async_computation.2 | async-start | bytes 2097152 | tf_op jit(solution)/shard_map/all_to_all | solution.py:27
  60.7 282.0 %all-gather.5.cloned.1.call-start = ((), (), s32[]{:S(2)}) async-start(), calls=%async_computation.4 | async-start | bytes 3145728 | tf_op jit(solution)/shard_map/all_gather | solution.py:69
  182.7 1.2 copy-start
  183.9 2.2 copy-start.3
Sparse Core Ops, SparseCore 0:
  55.4 127.1 all-gather.8
  184.8 125.0 all-gather.6
  311.4 31.2 all-gather.4
where the time goes:
time: 362 us; the launch traced here: 361 us
  waiting for transfers between devices  281 us (78%)
  matrix products  19.3 us (5%)
  local copies, waits for them, and re-layouts  18 us (5%)
  blocking collectives  17.9 us (5%)
  between operations  13.3 us (4%)
  starting transfers between devices  11.5 us (3%)
    all_gather x1, waiting for transfers between devices, local(): lax.all_gather(out_weight, 'seq', axis=0, tiled=True)  105 us
    all_gather x1, waiting for transfers between devices, carried_in(): gathered = lax.all_gather(part, axis)  104 us
    all_gather x1, waiting for transfers between devices, local(): gathered = lax.all_gather(returned, 'head', axis=0, tiled=True)  32.8 us
    all_to_all x1, blocking collectives, local(): lax.all_to_all(normed, 'head', split_axis=0, concat_axis=1, tiled=True)  17.9 us
    all_to_all x1, waiting for transfers between devices, local(): lax.all_to_all(values, 'head', split_axis=1, concat_axis=0, tiled=True)  13.1 us
    all_to_all x1, waiting for transfers between devices, local(): lax.all_to_all(queries, 'head', split_axis=1, concat_axis=0, tiled=True)  12.3 us
    all_to_all x1, waiting for transfers between devices, local(): lax.all_to_all(keys, 'head', split_axis=1, concat_axis=0, tiled=True)  12.2 us
    dot_general x1, matrix products, local(): jnp.dot(gathered, lax.all_gather(out_weight, 'seq', axis=0, tiled=True),...  11.9 us
  transfers between devices with their start and end apart: 6, of which 6 were waited for; matrix products, arithmetic and copies ran while one was open for 3% of the time, Pallas kernels for 0%

commit v1 on v0

--- a/solution.py
+++ b/solution.py
@@ -1,9 +1,41 @@
+import functools
 import jax
 import jax.numpy as jnp
 from jax import lax
 from jax.sharding import PartitionSpec as P
+from jax.lax import axis_index, axis_size, ppermute
 
 HEAD_DIM = 128
+
+
+def start_the_point(obj, ndim_at):
+    reply, local_part, response = (axis_size("seq"), axis_index("seq"), obj.shape[ndim_at])
+    heard = lax.dynamic_update_slice_in_dim(
+        jnp.zeros(
+            [dev_i * reply if t == ndim_at else dev_i for t, dev_i in enumerate(obj.shape)],
+            obj.dtype,
+        ),
+        obj,
+        local_part * response,
+        axis=ndim_at,
+    )
+    y1 = long_array = obj
+    for rr in range(1, reply // 2 + 1):
+        y1 = ppermute(y1, axis_name="seq", perm=[(t, (t + 1) % reply) for t in range(reply)])
+        heard = lax.dynamic_update_slice_in_dim(
+            heard, y1, (local_part - rr) % reply * response, axis=ndim_at
+        )
+        if 2 * rr < reply:
+            long_array = ppermute(
+                long_array, axis_name="seq", perm=[(t, (t - 1) % reply) for t in range(reply)]
+            )
+            heard = lax.dynamic_update_slice_in_dim(
+                heard, long_array, (local_part + rr) % reply * response, axis=ndim_at
+            )
+    return heard
+
+
+begin_skins_by_axis = functools.partial(start_the_point, ndim_at=0)
 
 
 def carried_in(part, axis, combine, identity):
@@ -67,11 +99,7 @@
     normed = normed.reshape(row_count, heads_dev * HEAD_DIM)
     returned = lax.all_to_all(normed, "head", split_axis=0, concat_axis=1, tiled=True)
     gathered = lax.all_gather(returned, "head", axis=0, tiled=True)
-    outcome = jnp.dot(
-        gathered,
-        lax.all_gather(out_weight, "seq", axis=0, tiled=True),
-        preferred_element_type=jnp.float32,
-    )
+    outcome = jnp.dot(gathered, begin_skins_by_axis(out_weight), preferred_element_type=jnp.float32)
     return outcome.astype(jnp.bfloat16)
 
 

time: 362 us -> 351 us (0.970)
  waiting for transfers between devices: 281 us -> 145 us
  starting transfers between devices: 11.5 us -> 110 us
  local copies, waits for them, and re-layouts: 18 us -> 59.6 us
  blocking collectives: 17.9 us -> 0 us
    all_gather x1 -> x0, waiting for transfers between devices: 105 us -> none  [local(): lax.all_gather(out_weight, 'seq', axis=0, tiled=True)]
    ppermute x0 -> x15, starting transfers between devices: none -> 95.3 us  [the longest x8 55.4 us: start_the_point(): ppermute(y1, axis_name='seq', perm=[(t, (t + 1) % reply) for t in range(r...]
    ppermute x0 -> x15, waiting for transfers between devices: none -> 91.9 us  [the longest x8 80.6 us: start_the_point(): ppermute(y1, axis_name='seq', perm=[(t, (t + 1) % reply) for t in range(r...]
    all_gather x1, waiting for transfers between devices: 104 us -> 17.3 us  [carried_in(): gathered = lax.all_gather(part, axis)]
    dynamic_update_slice x0 -> x16, local copies, waits for them, and re-layouts: none -> 32.5 us  [the longest x8 16.3 us: start_the_point(): lax.dynamic_update_slice_in_dim(heard, y1, (local_part - rr) % reply * re...]
    all_gather x1, waiting for transfers between devices: 32.8 us -> 4.32 us  [local(): gathered = lax.all_gather(returned, 'head', axis=0, tiled=True)]
    all_to_all x1 -> x0, blocking collectives: 17.9 us -> none  [local(): lax.all_to_all(normed, 'head', split_axis=0, concat_axis=1, tiled=True)]
    all_to_all x1, waiting for transfers between devices: 12.3 us -> 1.85 us  [local(): lax.all_to_all(queries, 'head', split_axis=1, concat_axis=0, tiled=True)]
  transfers between devices with their start and end apart: 6 -> 21, of which waited for: 6 -> 14; matrix products, arithmetic and copies ran while one was open for 3% -> 15% of each run, Pallas kernels for 0% -> 0%
where the time goes in v1:
time: 351 us; the launch traced here: 349 us
  waiting for transfers between devices  145 us (41%)
  starting transfers between devices  110 us (31%)
  local copies, waits for them, and re-layouts  59.6 us (17%)
  matrix products  19.7 us (6%)
  between operations  13.9 us (4%)
    ppermute x8, waiting for transfers between devices, start_the_point(): ppermute(y1, axis_name='seq', perm=[(t, (t + 1) % reply) for t in range(r...  80.6 us
    ppermute x8, starting transfers between devices, start_the_point(): ppermute(y1, axis_name='seq', perm=[(t, (t + 1) % reply) for t in range(r...  55.4 us
    ppermute x7, starting transfers between devices, start_the_point(): ppermute(long_array, axis_name='seq', perm=[(t, (t - 1) % reply) for t in...  40 us
    all_gather x1, waiting for transfers between devices, carried_in(): gathered = lax.all_gather(part, axis)  17.3 us
    dynamic_update_slice x8, local copies, waits for them, and re-layouts, start_the_point(): lax.dynamic_update_slice_in_dim(heard, y1, (local_part - rr) % reply * re...  16.3 us
    dynamic_update_slice x7, local copies, waits for them, and re-layouts, start_the_point(): lax.dynamic_update_slice_in_dim(heard, long_array, (local_part + rr) % re...  15.1 us
    all_to_all x1, waiting for transfers between devices, local(): lax.all_to_all(keys, 'head', split_axis=1, concat_axis=0, tiled=True)  12.2 us
    all_to_all x1, waiting for transfers between devices, local(): lax.all_to_all(values, 'head', split_axis=1, concat_axis=0, tiled=True)  12.2 us
  transfers between devices with their start and end apart: 21, of which 14 were waited for; matrix products, arithmetic and copies ran while one was open for 15% of the time, Pallas kernels for 0%

profile of v1, /device:TPU:0, one launch (start us, length us, event | category | flops | bytes accessed | tf_op | source)
XLA Modules:
  0.0 349.2 jit_solution(17798399090590680699)
XLA Ops:
  6.5 2.3 copy.44
  8.8 4.2 %all-to-all-start.1 = ((bf16[128,2,2048]{2,0,1:T(8,128)(2,1)}), bf16[128,2,2048]{2,0,1:T(8,128)(2,1)S(1)}, u32[]{:S(2)}, u32[]{:S(2)}) async-start(bf16[128,2,2048]{2,0,1:T(8,128)(2,1)} %bitcast.38), calls=%async_computation.1 | async-start | bytes 2097152 | tf_op jit(solution)/shard_map/all_to_all | solution.py:61
  13.0 2.3 copy.17
  15.3 12.2 %all-to-all-done.1 = bf16[128,2,2048]{2,0,1:T(8,128)(2,1)S(1)} async-done(((bf16[128,2,2048]{2,0,1:T(8,128)(2,1)}), bf16[128,2,2048]{2,0,1:T(8,128)(2,1)S(1)}, u32[]{:S(2)}, u32[]{:S(2)}) %all-to-all-start.1) | async-done | bytes 1048608 | tf_op jit(solution)/shard_map/all_to_all | solution.py:61
  27.5 3.6 %all-to-all-start = ((bf16[128,2,2048]{0,2,1:T(8,128)(2,1)}), bf16[128,2,2048]{0,2,1:T(8,128)(2,1)S(1)}, u32[]{:S(2)}, u32[]{:S(2)}) async-start(bf16[128,2,2048]{0,2,1:T(8,128)(2,1)} %bitcast.1), calls=%async_computation | async-start | bytes 2097152 | tf_op jit(solution)/shard_map/all_to_all | solution.py:60
  32.1 12.2 %all-to-all-done = bf16[128,2,2048]{0,2,1:T(8,128)(2,1)S(1)} async-done(((bf16[128,2,2048]{0,2,1:T(8,128)(2,1)}), bf16[128,2,2048]{0,2,1:T(8,128)(2,1)S(1)}, u32[]{:S(2)}, u32[]{:S(2)}) %all-to-all-start) | async-done | bytes 1048608 | tf_op jit(solution)/shard_map/all_to_all | solution.py:60
  44.4 8.6 %copy.18 = bf16[2,128,2048]{1,0,2:T(2,128)(2,1)S(1)} copy(bf16[2,128,2048]{1,2,0:T(8,128)(2,1)S(1)} %bitcast.45) | data formatting | bytes 2097152 | tf_op jit(solution)/shard_map/all_to_all | solution.py:60
  53.7 1.4 fusion.6
  55.3 4.4 %collective-permute-start.1 = (bf16[256,2048]{1,0:T(8,128)(2,1)}, bf16[256,2048]{1,0:T(8,128)(2,1)S(1)}, u32[]{:S(2)}, u32[]{:S(2)}) collective-permute-start(bf16[256,2048]{1,0:T(8,128)(2,1)} %param.10), channel_id=1, source_target_pairs={{0,30},{2,0},{4,2},{6,4},{8,6},{10,8},{12,10},{14,12},{16,14},{18,... | collective-permute-start | bytes 3145736 | tf_op jit(solution)/shard_map/ppermute | solution.py:29
  59.7 17.5 %collective-permute-done = bf16[256,2048]{1,0:T(8,128)(2,1)S(1)} collective-permute-done((bf16[256,2048]{1,0:T(8,128)(2,1)}, bf16[256,2048]{1,0:T(8,128)(2,1)S(1)}, u32[]{:S(2)}, u32[]{:S(2)}) %collective-permute-start) | collective-permute-done | bytes 1048608 | tf_op jit(solution)/shard_map/ppermute | solution.py:24
  77.2 14.0 %collective-permute-start.2 = (bf16[256,2048]{1,0:T(8,128)(2,1)S(1)}, bf16[256,2048]{1,0:T(8,128)(2,1)S(1)}, u32[]{:S(2)}, u32[]{:S(2)}) collective-permute-start(bf16[256,2048]{1,0:T(8,128)(2,1)S(1)} %collective-permute-done), channel_id=1, source_target_pairs={{0,2},{2,4},{4,6},{6,8},{8,10},{10,12},{12,14},{14,16},{16,18},{18... | collective-permute-start | bytes 3145736 | tf_op jit(solution)/shard_map/ppermute | solution.py:24
  91.3 25.3 %collective-permute-done.2 = bf16[256,2048]{1,0:T(8,128)(2,1)S(1)} collective-permute-done((bf16[256,2048]{1,0:T(8,128)(2,1)S(1)}, bf16[256,2048]{1,0:T(8,128)(2,1)S(1)}, u32[]{:S(2)}, u32[]{:S(2)}) %collective-permute-start.2) | collective-permute-done | bytes 1048608 | tf_op jit(solution)/shard_map/ppermute | solution.py:24
  117.7 4.7 %collective-permute-start.5 = (bf16[256,2048]{1,0:T(8,128)(2,1)S(1)}, bf16[256,2048]{1,0:T(8,128)(2,1)}, u32[]{:S(2)}, u32[]{:S(2)}) collective-permute-start(bf16[256,2048]{1,0:T(8,128)(2,1)S(1)} %collective-permute-done.3), channel_id=1, source_target_pairs={{0,30},{2,0},{4,2},{6,4},{8,6},{10,8},{12,10},{14,12},{16,14},{18,... | collective-permute-start | bytes 3145736 | tf_op jit(solution)/shard_map/ppermute | solution.py:29
  122.4 26.1 %collective-permute-done.4 = bf16[256,2048]{1,0:T(8,128)(2,1)} collective-permute-done((bf16[256,2048]{1,0:T(8,128)(2,1)S(1)}, bf16[256,2048]{1,0:T(8,128)(2,1)}, u32[]{:S(2)}, u32[]{:S(2)}) %collective-permute-start.4) | collective-permute-done | bytes 1048608 | tf_op jit(solution)/shard_map/ppermute | solution.py:24
  149.1 8.1 %collective-permute-done.5 = bf16[256,2048]{1,0:T(8,128)(2,1)} collective-permute-done((bf16[256,2048]{1,0:T(8,128)(2,1)S(1)}, bf16[256,2048]{1,0:T(8,128)(2,1)}, u32[]{:S(2)}, u32[]{:S(2)}) %collective-permute-start.5) | collective-permute-done | bytes 1048608 | tf_op jit(solution)/shard_map/ppermute | solution.py:29
  157.1 4.7 %collective-permute-start.7 = (bf16[256,2048]{1,0:T(8,128)(2,1)}, bf16[256,2048]{1,0:T(8,128)(2,1)}, u32[]{:S(2)}, u32[]{:S(2)}) collective-permute-start(bf16[256,2048]{1,0:T(8,128)(2,1)} %collective-permute-done.5), channel_id=1, source_target_pairs={{0,30},{2,0},{4,2},{6,4},{8,6},{10,8},{12,10},{14,12},{16,14},{18,... | collective-permute-start | bytes 3145736 | tf_op jit(solution)/shard_map/ppermute | solution.py:29
  161.9 2.3 copy.43
  164.2 3.6 %all-to-all-start.2 = ((bf16[128,2,2048]{2,0,1:T(8,128)(2,1)}), bf16[128,2,2048]{2,0,1:T(8,128)(2,1)S(1)}, u32[]{:S(2)}, u32[]{:S(2)}) async-start(bf16[128,2,2048]{2,0,1:T(8,128)(2,1)} %bitcast.42), calls=%async_computation.2 | async-start | bytes 2097152 | tf_op jit(solution)/shard_map/all_to_all | solution.py:59
  168.1 6.1 %broadcast_in_dim.22 = bf16[4096,2048]{1,0:T(8,128)(2,1)} broadcast(bf16[]{:T(256)} %constant.110.clone.1), dimensions={} | broadcast | bytes 16777218 | tf_op jit(solution)/shard_map/broadcast_in_dim | solution.py:14
  175.3 1.9 all-to-all-done.2
  177.1 1.2 copy.33
  178.3 6.1 %collective-permute-done.6 = bf16[256,2048]{1,0:T(8,128)(2,1)} collective-permute-done((bf16[256,2048]{1,0:T(8,128)(2,1)}, bf16[256,2048]{1,0:T(8,128)(2,1)}, u32[]{:S(2)}, u32[]{:S(2)}) %collective-permute-start.6) | collective-permute-done | bytes 1048608 | tf_op jit(solution)/shard_map/ppermute | solution.py:24
  184.4 17.6 %collective-permute-start.8 = (bf16[256,2048]{1,0:T(8,128)(2,1)}, bf16[256,2048]{1,0:T(8,128)(2,1)}, u32[]{:S(2)}, u32[]{:S(2)}) collective-permute-start(bf16[256,2048]{1,0:T(8,128)(2,1)} %collective-permute-done.6), channel_id=1, source_target_pairs={{0,2},{2,4},{4,6},{6,8},{8,10},{10,12},{12,14},{14,16},{16,18},{18... | collective-permute-start | bytes 3145736 | tf_op jit(solution)/shard_map/ppermute | solution.py:24
  202.1 3.9 %fusion = f32[16,256,128]{1,2,0:T(8,128)} fusion(bf16[256,16,128]{0,2,1:T(8,128)(2,1)S(1)} %copy.26, bf16[256,16,128]{0,2,1:T(8,128)(2,1)S(1)} %reshape.42, pred[256,256]{1,0:T(8,128)(4,1)S(1)} %iota_compare_fusion, bf16[256,16,128]{2,1,0:T(8,128)(2,1)} %bitcast.47), kind=kOutput, calls=%fused_computation.6 | convolution fusion | flops 538968064 | bytes 5308416 | tf_op jit(solution)/shard_map/hts,she->the/dot_general | solution.py:90
  206.0 2.4 constant_dynamic-update-slice_fusion.14
  208.4 2.3 constant_dynamic-update-slice_fusion.13
  210.7 2.3 constant_dynamic-update-slice_fusion.12
  213.0 21.3 %collective-permute-start.10 = (bf16[256,2048]{1,0:T(8,128)(2,1)}, bf16[256,2048]{1,0:T(8,128)(2,1)}, u32[]{:S(2)}, u32[]{:S(2)}) collective-permute-start(bf16[256,2048]{1,0:T(8,128)(2,1)} %collective-permute-done.8), channel_id=1, source_target_pairs={{0,2},{2,4},{4,6},{6,8},{8,10},{10,12},{12,14},{14,16},{16,18},{18... | collective-permute-start | bytes 3145736 | tf_op jit(solution)/shard_map/ppermute | solution.py:24
  234.3 17.3 %all-gather.6.cloned.1.call-done = f32[256,128,128]{2,1,0:T(8,128)} async-done(((f32[16,128,128]{2,1,0:T(8,128)}), f32[256,128,128]{2,1,0:T(8,128)}) %all-gather.6.cloned.1.call-update) | async-done | bytes 16777232 | tf_op jit(solution)/shard_map/all_gather | solution.py:43
  251.8 2.5 multiply_reduce_fusion
  256.1 3.6 %all-to-all-start.3 = ((bf16[2,128,2048]{1,2,0:T(8,128)(2,1)}), bf16[2,128,2048]{1,2,0:T(8,128)(2,1)S(1)}, u32[]{:S(2)}, u32[]{:S(2)}) async-start(bf16[2,128,2048]{1,2,0:T(8,128)(2,1)} %copy.27), calls=%async_computation.3 | async-start | bytes 2097152 | tf_op jit(solution)/shard_map/all_to_all | solution.py:100
  259.7 2.3 constant_dynamic-update-slice_fusion.11
  262.1 1.7 collective-permute-start.12
  263.8 2.3 constant_dynamic-update-slice_fusion.10
  266.1 2.3 constant_dynamic-update-slice_fusion.9
  268.4 5.5 %all-to-all-done.3 = bf16[2,128,2048]{1,2,0:T(8,128)(2,1)S(1)} async-done(((bf16[2,128,2048]{1,2,0:T(8,128)(2,1)}), bf16[2,128,2048]{1,2,0:T(8,128)(2,1)S(1)}, u32[]{:S(2)}, u32[]{:S(2)}) %all-to-all-start.3) | async-done | bytes 1048608 | tf_op jit(solution)/shard_map/all_to_all | solution.py:100
  274.9 2.3 constant_dynamic-update-slice_fusion.8
  277.2 2.4 constant_dynamic-update-slice_fusion.7
  279.6 26.1 %collective-permute-start.13 = (bf16[256,2048]{1,0:T(8,128)(2,1)}, bf16[256,2048]{1,0:T(8,128)(2,1)S(1)}, u32[]{:S(2)}, u32[]{:S(2)}) collective-permute-start(bf16[256,2048]{1,0:T(8,128)(2,1)} %collective-permute-done.11), channel_id=1, source_target_pairs={{0,30},{2,0},{4,2},{6,4},{8,6},{10,8},{12,10},{14,12},{16,14},{18,... | collective-permute-start | bytes 3145736 | tf_op jit(solution)/shard_map/ppermute | solution.py:29
  305.7 2.4 constant_dynamic-update-slice_fusion.6
  308.1 2.3 constant_dynamic-update-slice_fusion.5
  310.4 2.3 constant_dynamic-update-slice_fusion.4
  312.7 2.3 constant_dynamic-update-slice_fusion.3
  316.2 2.2 collective-permute-done.13
  318.4 1.2 constant_dynamic-update-slice_fusion.1
  319.5 5.5 %collective-permute-done.14 = bf16[256,2048]{1,0:T(8,128)(2,1)S(1)} collective-permute-done((bf16[256,2048]{1,0:T(8,128)(2,1)S(1)}, bf16[256,2048]{1,0:T(8,128)(2,1)S(1)}, u32[]{:S(2)}, u32[]{:S(2)}) %collective-permute-start.14) | collective-permute-done | bytes 1048608 | tf_op jit(solution)/shard_map/ppermute | solution.py:24
  326.2 4.3 %all-gather.4.cloned.1.call-done = bf16[256,4096]{0,1:T(8,128)(2,1)} async-done(((bf16[128,4096]{0,1:T(8,128)(2,1)}), bf16[256,4096]{0,1:T(8,128)(2,1)}) %all-gather.4.cloned.1.call-update) | async-done | bytes 2097168 | tf_op jit(solution)/shard_map/all_gather | solution.py:101
  330.5 11.9 %convolution_convert_fusion = bf16[256,2048]{1,0:T(8,128)(2,1)} fusion(bf16[256,4096]{0,1:T(8,128)(2,1)} %all-gather.4.cloned.1.call-done, bf16[4096,2048]{1,0:T(8,128)(2,1)} %constant_dynamic-update-slice_fusion), kind=kOutput, calls=%fused_computation.2 | convolution fusion | flops 4295491584 | bytes 19922944 | tf_op jit(solution)/shard_map/dot_general | solution.py:102
  (46 shorter events, 9.7 us)
Async XLA Ops:
  8.8 18.6 %all-to-all-start.1 = ((bf16[128,2,2048]{2,0,1:T(8,128)(2,1)}), bf16[128,2,2048]{2,0,1:T(8,128)(2,1)S(1)}, u32[]{:S(2)}, u32[]{:S(2)}) async-start(bf16[128,2,2048]{2,0,1:T(8,128)(2,1)} %bitcast.38), calls=%async_computation.1 | async-start | bytes 2097152 | tf_op jit(solution)/shard_map/all_to_all | solution.py:61
  27.5 16.9 %all-to-all-start = ((bf16[128,2,2048]{0,2,1:T(8,128)(2,1)}), bf16[128,2,2048]{0,2,1:T(8,128)(2,1)S(1)}, u32[]{:S(2)}, u32[]{:S(2)}) async-start(bf16[128,2,2048]{0,2,1:T(8,128)(2,1)} %bitcast.1), calls=%async_computation | async-start | bytes 2097152 | tf_op jit(solution)/shard_map/all_to_all | solution.py:60
  31.1 220.6 %all-gather.6.cloned.1.call-start = ((), (), s32[]{:S(2)}) async-start(), calls=%async_computation.5 | async-start | bytes 17825792 | tf_op jit(solution)/shard_map/all_gather | solution.py:43
  55.2 22.0 %collective-permute-start = (bf16[256,2048]{1,0:T(8,128)(2,1)}, bf16[256,2048]{1,0:T(8,128)(2,1)S(1)}, u32[]{:S(2)}, u32[]{:S(2)}) collective-permute-start(bf16[256,2048]{1,0:T(8,128)(2,1)} %param.10), channel_id=1, source_target_pairs={{0,2},{2,4},{4,6},{6,8},{8,10},{10,12},{12,14},{14,16},{16,18},{18... | collective-permute-start | bytes 3145736 | tf_op jit(solution)/shard_map/ppermute | solution.py:24
  55.3 36.0 %collective-permute-start.1 = (bf16[256,2048]{1,0:T(8,128)(2,1)}, bf16[256,2048]{1,0:T(8,128)(2,1)S(1)}, u32[]{:S(2)}, u32[]{:S(2)}) collective-permute-start(bf16[256,2048]{1,0:T(8,128)(2,1)} %param.10), channel_id=1, source_target_pairs={{0,30},{2,0},{4,2},{6,4},{8,6},{10,8},{12,10},{14,12},{16,14},{18,... | collective-permute-start | bytes 3145736 | tf_op jit(solution)/shard_map/ppermute | solution.py:29
  77.2 79.9 %copy-start.3 = (bf16[256,2048]{1,0:T(8,128)(2,1)}, bf16[256,2048]{1,0:T(8,128)(2,1)S(1)}, u32[]{:S(2)}) copy-start(bf16[256,2048]{1,0:T(8,128)(2,1)S(1)} %collective-permute-done) | copy-start | bytes 3145732
  77.2 39.4 %collective-permute-start.2 = (bf16[256,2048]{1,0:T(8,128)(2,1)S(1)}, bf16[256,2048]{1,0:T(8,128)(2,1)S(1)}, u32[]{:S(2)}, u32[]{:S(2)}) collective-permute-start(bf16[256,2048]{1,0:T(8,128)(2,1)S(1)} %collective-permute-done), channel_id=1, source_target_pairs={{0,2},{2,4},{4,6},{6,8},{8,10},{10,12},{12,14},{14,16},{16,18},{18... | collective-permute-start | bytes 3145736 | tf_op jit(solution)/shard_map/ppermute | solution.py:24
  91.3 70.6 %copy-start.4 = (bf16[256,2048]{1,0:T(8,128)(2,1)}, bf16[256,2048]{1,0:T(8,128)(2,1)S(1)}, u32[]{:S(2)}) copy-start(bf16[256,2048]{1,0:T(8,128)(2,1)S(1)} %collective-permute-done.1) | copy-start | bytes 3145732
  91.3 26.4 %collective-permute-start.3 = (bf16[256,2048]{1,0:T(8,128)(2,1)S(1)}, bf16[256,2048]{1,0:T(8,128)(2,1)S(1)}, u32[]{:S(2)}, u32[]{:S(2)}) collective-permute-start(bf16[256,2048]{1,0:T(8,128)(2,1)S(1)} %collective-permute-done.1), channel_id=1, source_target_pairs={{0,30},{2,0},{4,2},{6,4},{8,6},{10,8},{12,10},{14,12},{16,14},{18,... | collective-permute-start | bytes 3145736 | tf_op jit(solution)/shard_map/ppermute | solution.py:29
  116.6 45.3 %copy-start.5 = (bf16[256,2048]{1,0:T(8,128)(2,1)}, bf16[256,2048]{1,0:T(8,128)(2,1)S(1)}, u32[]{:S(2)}) copy-start(bf16[256,2048]{1,0:T(8,128)(2,1)S(1)} %collective-permute-done.2) | copy-start | bytes 3145732
  116.6 31.9 %collective-permute-start.4 = (bf16[256,2048]{1,0:T(8,128)(2,1)S(1)}, bf16[256,2048]{1,0:T(8,128)(2,1)}, u32[]{:S(2)}, u32[]{:S(2)}) collective-permute-start(bf16[256,2048]{1,0:T(8,128)(2,1)S(1)} %collective-permute-done.2), channel_id=1, source_target_pairs={{0,2},{2,4},{4,6},{6,8},{8,10},{10,12},{12,14},{14,16},{16,18},{18... | collective-permute-start | bytes 3145736 | tf_op jit(solution)/shard_map/ppermute | solution.py:24
  117.7 46.5 %copy-start.2 = (bf16[256,2048]{1,0:T(8,128)(2,1)}, bf16[256,2048]{1,0:T(8,128)(2,1)S(1)}, u32[]{:S(2)}) copy-start(bf16[256,2048]{1,0:T(8,128)(2,1)S(1)} %collective-permute-done.3) | copy-start | bytes 3145732
  117.7 39.5 %collective-permute-start.5 = (bf16[256,2048]{1,0:T(8,128)(2,1)S(1)}, bf16[256,2048]{1,0:T(8,128)(2,1)}, u32[]{:S(2)}, u32[]{:S(2)}) collective-permute-start(bf16[256,2048]{1,0:T(8,128)(2,1)S(1)} %collective-permute-done.3), channel_id=1, source_target_pairs={{0,30},{2,0},{4,2},{6,4},{8,6},{10,8},{12,10},{14,12},{16,14},{18,... | collective-permute-start | bytes 3145736 | tf_op jit(solution)/shard_map/ppermute | solution.py:29
  148.5 35.9 %collective-permute-start.6 = (bf16[256,2048]{1,0:T(8,128)(2,1)}, bf16[256,2048]{1,0:T(8,128)(2,1)}, u32[]{:S(2)}, u32[]{:S(2)}) collective-permute-start(bf16[256,2048]{1,0:T(8,128)(2,1)} %collective-permute-done.4), channel_id=1, source_target_pairs={{0,2},{2,4},{4,6},{6,8},{8,10},{10,12},{12,14},{14,16},{16,18},{18... | collective-permute-start | bytes 3145736 | tf_op jit(solution)/shard_map/ppermute | solution.py:24
  157.1 44.9 %collective-permute-start.7 = (bf16[256,2048]{1,0:T(8,128)(2,1)}, bf16[256,2048]{1,0:T(8,128)(2,1)}, u32[]{:S(2)}, u32[]{:S(2)}) collective-permute-start(bf16[256,2048]{1,0:T(8,128)(2,1)} %collective-permute-done.5), channel_id=1, source_target_pairs={{0,30},{2,0},{4,2},{6,4},{8,6},{10,8},{12,10},{14,12},{16,14},{18,... | collective-permute-start | bytes 3145736 | tf_op jit(solution)/shard_map/ppermute | solution.py:29
  164.2 13.0 %all-to-all-start.2 = ((bf16[128,2,2048]{2,0,1:T(8,128)(2,1)}), bf16[128,2,2048]{2,0,1:T(8,128)(2,1)S(1)}, u32[]{:S(2)}, u32[]{:S(2)}) async-start(bf16[128,2,2048]{2,0,1:T(8,128)(2,1)} %bitcast.42), calls=%async_computation.2 | async-start | bytes 2097152 | tf_op jit(solution)/shard_map/all_to_all | solution.py:59
  168.1 6.2 %copy-start.1 = (bf16[256,2048]{1,0:T(8,128)(2,1)S(1)}, bf16[256,2048]{1,0:T(8,128)(2,1)}, u32[]{:S(2)}) copy-start(bf16[256,2048]{1,0:T(8,128)(2,1)} %param.10) | copy-start | bytes 3145732
  184.4 28.6 %collective-permute-start.8 = (bf16[256,2048]{1,0:T(8,128)(2,1)}, bf16[256,2048]{1,0:T(8,128)(2,1)}, u32[]{:S(2)}, u32[]{:S(2)}) collective-permute-start(bf16[256,2048]{1,0:T(8,128)(2,1)} %collective-permute-done.6), channel_id=1, source_target_pairs={{0,2},{2,4},{4,6},{6,8},{8,10},{10,12},{12,14},{14,16},{16,18},{18... | collective-permute-start | bytes 3145736 | tf_op jit(solution)/shard_map/ppermute | solution.py:24
  202.1 32.3 %collective-permute-start.9 = (bf16[256,2048]{1,0:T(8,128)(2,1)}, bf16[256,2048]{1,0:T(8,128)(2,1)}, u32[]{:S(2)}, u32[]{:S(2)}) collective-permute-start(bf16[256,2048]{1,0:T(8,128)(2,1)} %collective-permute-done.7), channel_id=1, source_target_pairs={{0,30},{2,0},{4,2},{6,4},{8,6},{10,8},{12,10},{14,12},{16,14},{18,... | collective-permute-start | bytes 3145736 | tf_op jit(solution)/shard_map/ppermute | solution.py:29
  202.1 52.2 %copy-start.6 = (f32[2048]{0:T(1024)S(1)}, f32[2048]{0:T(1024)}, u32[]{:S(2)}) copy-start(f32[2048]{0:T(1024)} %param.11) | copy-start | bytes 24580
  213.0 49.0 %collective-permute-start.10 = (bf16[256,2048]{1,0:T(8,128)(2,1)}, bf16[256,2048]{1,0:T(8,128)(2,1)}, u32[]{:S(2)}, u32[]{:S(2)}) collective-permute-start(bf16[256,2048]{1,0:T(8,128)(2,1)} %collective-permute-done.8), channel_id=1, source_target_pairs={{0,2},{2,4},{4,6},{6,8},{8,10},{10,12},{12,14},{14,16},{16,18},{18... | collective-permute-start | bytes 3145736 | tf_op jit(solution)/shard_map/ppermute | solution.py:24
  234.3 45.3 %collective-permute-start.11 = (bf16[256,2048]{1,0:T(8,128)(2,1)}, bf16[256,2048]{1,0:T(8,128)(2,1)}, u32[]{:S(2)}, u32[]{:S(2)}) collective-permute-start(bf16[256,2048]{1,0:T(8,128)(2,1)} %collective-permute-done.9), channel_id=1, source_target_pairs={{0,30},{2,0},{4,2},{6,4},{8,6},{10,8},{12,10},{14,12},{16,14},{18,... | collective-permute-start | bytes 3145736 | tf_op jit(solution)/shard_map/ppermute | solution.py:29
  256.1 17.8 %all-to-all-start.3 = ((bf16[2,128,2048]{1,2,0:T(8,128)(2,1)}), bf16[2,128,2048]{1,2,0:T(8,128)(2,1)S(1)}, u32[]{:S(2)}, u32[]{:S(2)}) async-start(bf16[2,128,2048]{1,2,0:T(8,128)(2,1)} %copy.27), calls=%async_computation.3 | async-start | bytes 2097152 | tf_op jit(solution)/shard_map/all_to_all | solution.py:100
  259.7 70.8 %all-gather.4.cloned.1.call-start = ((), (), s32[]{:S(2)}) async-start(), calls=%async_computation.4 | async-start | bytes 3145728 | tf_op jit(solution)/shard_map/all_gather | solution.py:101
  262.1 46.0 %collective-permute-start.12 = (bf16[256,2048]{1,0:T(8,128)(2,1)}, bf16[256,2048]{1,0:T(8,128)(2,1)S(1)}, u32[]{:S(2)}, u32[]{:S(2)}) collective-permute-start(bf16[256,2048]{1,0:T(8,128)(2,1)} %collective-permute-done.10), channel_id=1, source_target_pairs={{0,2},{2,4},{4,6},{6,8},{8,10},{10,12},{12,14},{14,16},{16,18},{18... | collective-permute-start | bytes 3145736 | tf_op jit(solution)/shard_map/ppermute | solution.py:24
  273.9 1.0 copy-start
  279.6 38.7 %collective-permute-start.13 = (bf16[256,2048]{1,0:T(8,128)(2,1)}, bf16[256,2048]{1,0:T(8,128)(2,1)S(1)}, u32[]{:S(2)}, u32[]{:S(2)}) collective-permute-start(bf16[256,2048]{1,0:T(8,128)(2,1)} %collective-permute-done.11), channel_id=1, source_target_pairs={{0,30},{2,0},{4,2},{6,4},{8,6},{10,8},{12,10},{14,12},{16,14},{18,... | collective-permute-start | bytes 3145736 | tf_op jit(solution)/shard_map/ppermute | solution.py:29
  308.1 16.9 %collective-permute-start.14 = (bf16[256,2048]{1,0:T(8,128)(2,1)S(1)}, bf16[256,2048]{1,0:T(8,128)(2,1)S(1)}, u32[]{:S(2)}, u32[]{:S(2)}) collective-permute-start(bf16[256,2048]{1,0:T(8,128)(2,1)S(1)} %collective-permute-done.12), channel_id=1, source_target_pairs={{0,2},{2,4},{4,6},{6,8},{8,10},{10,12},{12,14},{14,16},{16,18},{18... | collective-permute-start | bytes 3145736 | tf_op jit(solution)/shard_map/ppermute | solution.py:24
Sparse Core Ops, SparseCore 0:
  55.3 196.2 all-gather.5
  275.0 55.4 all-gather.3
